TPU v7x, 256 devices: a whole 4x4x8 slice. The times are simulated.
256 devices in a mesh: gx: 16 (over z, core), gy: 16 (over y, x).
Axes of the slice: x: 4, y: 4, z: 8, core: 2. Of those that a mesh axis runs over, the one named last changes fastest.
Arguments:
- field: float32 [64, 4096, 128], P('gy', 'gx'), may hold values from -5 to 5
- courant: float32 [3, 64, 4096, 128], P(None, 'gy', 'gx'), may hold values from -2.5 to 2.5
- diffusion_number: float32 [64, 4096, 128], P('gy', 'gx'), may hold values from 65536 to 1310720
Outputs:
- solved: float32 [64, 4096, 128], P('gy', 'gx')
All inputs are finite; a program needn't handle non-finite values.
Results may differ from a plain program's by a relative error of at most 0.0013.
Values sent between devices are 32-bit elements; how exact they have to be, the bound alone decides.
No kernel may reach another device: no remote copies, remote signals or barrier semaphores. Data moves between devices by JAX's collectives and lax.ppermute only.
A program may use at most 64 MiB of HBM per device.

v0:
```python
import jax
import jax.numpy as jnp
from jax import lax
from jax.sharding import PartitionSpec as P


def padded_2(cells, sides, width, closed):
    for axis, dim in sides:
        count = lax.axis_size(axis)
        ends = count if closed else count - 1
        head = lax.slice_in_dim(cells, 0, width, axis=dim)
        tail = lax.slice_in_dim(cells, cells.shape[dim] - width, cells.shape[dim], axis=dim)
        cells = jnp.concatenate(
            [
                lax.ppermute(tail, axis, [(i, (i + 1) % count) for i in range(ends)]),
                cells,
                lax.ppermute(head, axis, [((i + 1) % count, i) for i in range(ends)]),
            ],
            axis=dim,
        )
    return cells


def difference_pair(padded, sweep_direction, length):
    shifted = [
        lax.slice_in_dim(padded, offset, offset + length, axis=sweep_direction)
        for offset in range(5)
    ]
    gradient = (8.0 * (shifted[3] - shifted[1]) - (shifted[4] - shifted[0])) / 12.0
    curvature = (
        16.0 * (shifted[3] + shifted[1]) - (shifted[4] + shifted[0]) - 30.0 * shifted[2]
    ) / 12.0
    return (gradient, curvature)


def build_rhs(field, courant, y_padded, x_padded):
    z_padded = jnp.concatenate([field[:, :, -2:], field, field[:, :, :2]], 2)
    grad_y, curve_y = difference_pair(y_padded, 0, field.shape[0])
    grad_x = difference_pair(x_padded, 1, field.shape[1])[0]
    grad_z, curve_z = difference_pair(z_padded, 2, field.shape[2])
    transport = courant[0] * grad_x + courant[1] * grad_y + courant[2] * grad_z
    return field - transport + 0.05 * (curve_y + curve_z) + 0.3 * field / (1.0 + field * field)


def rows_below(values, stride, fill, sweep_direction):
    length = values.shape[sweep_direction]
    filler = jnp.full_like(lax.slice_in_dim(values, 0, stride, axis=sweep_direction), fill)
    return jnp.concatenate(
        [filler, lax.slice_in_dim(values, 0, length - stride, axis=sweep_direction)],
        sweep_direction,
    )


def rows_above(values, stride, fill, sweep_direction):
    length = values.shape[sweep_direction]
    filler = jnp.full_like(
        lax.slice_in_dim(values, length - stride, length, axis=sweep_direction), fill
    )
    return jnp.concatenate(
        [lax.slice_in_dim(values, stride, length, axis=sweep_direction), filler], sweep_direction
    )


def combine_rows(own_rows, below_set, above_set):
    lower_band, main_diagonal, upper_band, right_hand_sides = own_rows
    low_sub, low_diag, low_super, low_rights = below_set
    high_sub, high_diag, high_super, high_rights = above_set
    factor_low = -lower_band / low_diag
    factor_high = -upper_band / high_diag
    new_sub = factor_low * low_sub
    new_super = factor_high * high_super
    new_diag = main_diagonal + factor_low * low_super + factor_high * high_sub
    new_rights = tuple(
        (
            value + factor_low * lower_value + factor_high * upper_value
            for value, lower_value, upper_value in zip(right_hand_sides, low_rights, high_rights)
        )
    )
    return (new_sub, new_diag, new_super, new_rights)


def parallel_cyclic_reduction(
    lower_band, main_diagonal, upper_band, right_hand_sides, sweep_direction
):
    length = main_diagonal.shape[sweep_direction]
    stride = 1
    while stride < length:
        below_set = (
            rows_below(lower_band, stride, 0.0, sweep_direction),
            rows_below(main_diagonal, stride, 1.0, sweep_direction),
            rows_below(upper_band, stride, 0.0, sweep_direction),
            tuple((rows_below(value, stride, 0.0, sweep_direction) for value in right_hand_sides)),
        )
        above_set = (
            rows_above(lower_band, stride, 0.0, sweep_direction),
            rows_above(main_diagonal, stride, 1.0, sweep_direction),
            rows_above(upper_band, stride, 0.0, sweep_direction),
            tuple((rows_above(value, stride, 0.0, sweep_direction) for value in right_hand_sides)),
        )
        lower_band, main_diagonal, upper_band, right_hand_sides = combine_rows(
            (lower_band, main_diagonal, upper_band, right_hand_sides), below_set, above_set
        )
        stride = stride * 2
    return tuple((value / main_diagonal for value in right_hand_sides))


def shards(field, courant, diffusion_number):
    y_padded = padded_2(field, (("gy", 0),), 2, True)
    x_padded = padded_2(field, (("gx", 1),), 2, False)
    rhs = build_rhs(field, courant, y_padded, x_padded)
    place = lax.axis_index("gx")
    device_count = lax.axis_size("gx")
    sub_full = -diffusion_number
    diag_full = 1.0 + 2.0 * diffusion_number
    super_full = -diffusion_number
    edge_zeros = jnp.zeros_like(rhs[:, 0:1])
    inner_zeros = jnp.zeros_like(rhs[:, 3:])
    sub_inner = jnp.concatenate([edge_zeros, sub_full[:, 2:-1]], 1)
    super_inner = jnp.concatenate([super_full[:, 1:-2], edge_zeros], 1)
    diag_inner = diag_full[:, 1:-1]
    first_unit = jnp.concatenate([-sub_full[:, 1:2], inner_zeros], 1)
    last_unit = jnp.concatenate([inner_zeros, -super_full[:, -2:-1]], 1)
    particular_solution, first_row_response, last_row_response = parallel_cyclic_reduction(
        sub_inner, diag_inner, super_inner, (rhs[:, 1:-1], first_unit, last_unit), 1
    )
    low_open = (place > 0).astype(jnp.float32)
    high_open = (place < device_count - 1).astype(jnp.float32)
    sub_first = sub_full[:, 0:1] * low_open
    diag_first = diag_full[:, 0:1] + super_full[:, 0:1] * first_row_response[:, 0:1]
    super_first = super_full[:, 0:1] * last_row_response[:, 0:1]
    right_first = rhs[:, 0:1] - super_full[:, 0:1] * particular_solution[:, 0:1]
    sub_last = sub_full[:, -1:] * first_row_response[:, -1:]
    diag_last = diag_full[:, -1:] + sub_full[:, -1:] * last_row_response[:, -1:]
    super_last = super_full[:, -1:] * high_open
    right_last = rhs[:, -1:] - sub_full[:, -1:] * particular_solution[:, -1:]
    reduced_sub = jnp.concatenate([sub_first, sub_last], 1)
    reduced_diag = jnp.concatenate([diag_first, diag_last], 1)
    reduced_super = jnp.concatenate([super_first, super_last], 1)
    reduced_right = jnp.concatenate([right_first, right_last], 1)
    gathered_lower_band, gathered_diagonal, gathered_upper_band, gathered_rhs = (
        lax.all_gather(reduced_sub, "gx", axis=1, tiled=True),
        lax.all_gather(reduced_diag, "gx", axis=1, tiled=True),
        lax.all_gather(reduced_super, "gx", axis=1, tiled=True),
        lax.all_gather(reduced_right, "gx", axis=1, tiled=True),
    )
    boundary_rows_gathered = parallel_cyclic_reduction(
        gathered_lower_band, gathered_diagonal, gathered_upper_band, (gathered_rhs,), 1
    )[0]
    ends = lax.dynamic_slice_in_dim(boundary_rows_gathered, 2 * place, 2, 1)
    interior = (
        particular_solution + first_row_response * ends[:, 0:1] + last_row_response * ends[:, 1:2]
    )
    return jnp.concatenate([ends[:, 0:1], interior, ends[:, 1:2]], 1)


def solution(mesh):
    in_specs = (P("gy", "gx", None), P(None, "gy", "gx", None), P("gy", "gx", None))
    out_specs = P("gy", "gx", None)
    return jax.shard_map(shards, mesh=mesh, in_specs=in_specs, out_specs=out_specs, check_vma=False)
```

profile of v0, /device:TPU:1, one launch (start us, length us, event | category | flops | bytes accessed | tf_op | source)
XLA Modules:
  0.0 117.3 jit_solution(6404665510396162908)
XLA Ops:
  0.0 1.4 %copy.19 = f32[4,256,128]{2,0,1:T(4,128)S(1)} copy(f32[4,256,128]{2,1,0:T(8,128)} %param.3) | data formatting | bytes 1048576 | tf_op args[0]
  1.4 4.9 %collective-permute-start.1 = (f32[4,2,128]{2,0,1:T(4,128)S(1)}, f32[4,2,128]{2,0,1:T(4,128)S(1)}, u32[]{:S(2)}, u32[]{:S(2)}) collective-permute-start(f32[4,2,128]{2,0,1:T(4,128)S(1)} %get-tuple-element.94), channel_id=1, source_target_pairs={{0,16},{16,32},{32,48},{48,64},{64,80},{80,96},{96,112},{112,128},... | collective-permute-start | bytes 12296 | tf_op jit(solution)/shard_map/ppermute | solution.py:15
  6.3 2.1 %collective-permute-start = (f32[4,2,128]{2,0,1:T(4,128)S(1)}, f32[4,2,128]{2,0,1:T(4,128)S(1)}, u32[]{:S(2)}, u32[]{:S(2)}) collective-permute-start(f32[4,2,128]{2,0,1:T(4,128)S(1)} %get-tuple-element.93), channel_id=1, source_target_pairs={{16,0},{32,16},{48,32},{64,48},{80,64},{96,80},{112,96},{128,112},... | collective-permute-start | bytes 12296 | tf_op jit(solution)/shard_map/ppermute | solution.py:17
  8.4 1.0 fusion.36
  9.4 4.9 %collective-permute-start.2 = (f32[2,256,128]{2,0,1:T(2,128)}, f32[2,256,128]{2,0,1:T(2,128)S(1)}, u32[]{:S(2)}, u32[]{:S(2)}) collective-permute-start(f32[2,256,128]{2,0,1:T(2,128)} %get-tuple-element.90), channel_id=1, source_target_pairs={{1,0},{2,1},{3,2},{4,3},{5,4},{6,5},{7,6},{8,7},{9,8},{10,9},{11,1... | collective-permute-start | bytes 786440 | tf_op jit(solution)/shard_map/ppermute | solution.py:17
  14.3 1.3 %fusion.37 = (f32[4,256,2]{2,0,1:T(4,128)}, f32[4,256,2]{2,0,1:T(4,128)}) fusion(f32[4,256,128]{2,0,1:T(4,128)S(1)} %copy.19), kind=kLoop, calls=%fused_computation.178 | loop fusion | bytes 32768 | tf_op jit(solution)/shard_map/slice | solution.py:37
  15.6 1.2 %fusion.32 = (f32[1,4,256,128]{3,2,1,0:T(8,128)}, f32[1,4,256,128]{3,2,1,0:T(8,128)}, f32[1,4,256,128]{3,2,1,0:T(8,128)}) fusion(f32[3,4,256,128]{3,2,1,0:T(8,128)S(1)} %copy-done.10), kind=kLoop, calls=%fused_computation.173 | loop fusion | bytes 3145728 | tf_op jit(solution)/shard_map/slice | solution.py:41
  17.4 1.2 %fusion.33 = (f32[4,253,128]{2,0,1:T(4,128)S(1)}, f32[4,253,128]{2,0,1:T(4,128)S(1)}, f32[4,253,128]{2,0,1:T(4,128)}, f32[4,253,128]{2,0,1:T(4,128)}) fusion(f32[4,256,128]{2,0,1:T(4,128)S(1)} %get-tuple-element.85, f32[4,256,128]{2,0,1:T(4,128)S(1)} %get-tuple-element.86), kind=kLoop, calls=%fused_computation.174 | loop fusion | bytes 4145152 | tf_op jit(solution)/shard_map/slice | solution.py:119
  18.6 0.8 pad_slice_fusion.10
  19.5 1.1 pad_slice_fusion.8
  22.0 2.4 %collective-permute-done.3 = f32[2,256,128]{2,0,1:T(2,128)} collective-permute-done((f32[2,256,128]{2,0,1:T(2,128)}, f32[2,256,128]{2,0,1:T(2,128)}, u32[]{:S(2)}, u32[]{:S(2)}) %collective-permute-start.3) | collective-permute-done | bytes 262176 | tf_op jit(solution)/shard_map/ppermute | solution.py:15
  24.4 4.7 %fusion.11 = f32[4,256,128]{2,0,1:T(4,128)S(1)} fusion(f32[4,256,128]{2,0,1:T(4,128)S(1)} %copy.19, f32[4,258,128]{2,0,1:T(4,128)S(1)} %get-tuple-element.96, f32[4,258,128]{2,0,1:T(4,128)S(1)} %constant_dynamic-update-slice_fusion, f32[1,4,256,128]{3,2,1,0:T(8,128)} %get-tuple-element.51, f32[1,4,256,128]{3,2,1,0:T(8,128)} %get-tuple-element.50, ...), kind=kLoop, calls=%fused_computation.28 | loop fusion | flops 6291456 | bytes 5259264 | tf_op jit(solution)/shard_map/add | solution.py:42
  29.3 0.9 copy-done.4
  32.7 1.9 %multiply_add_fusion.26 = (f32[4,254,128]{2,0,1:T(4,128)S(1)}, f32[4,254,128]{2,0,1:T(4,128)S(1)}, f32[4,254,128]{2,0,1:T(4,128)S(1)}, f32[4,254,128]{2,0,1:T(4,...) fusion(f32[4,252,128]{2,0,1:T(4,128)S(1)} %get-tuple-element.178, ...), kind=kLoop, calls=%fused_computation.96 | loop fusion | flops 2340864 | bytes 9343992 | tf_op jit(solution)/shard_map/add | solution.py:75
  35.8 1.3 %multiply_add_fusion.24 = (f32[4,254,128]{2,0,1:T(4,128)S(1)}, f32[4,254,128]{2,0,1:T(4,128)S(1)}, f32[4,254,128]{2,0,1:T(4,128)S(1)}, f32[4,254,128]{2,0,1:T(4,...) fusion(f32[4,250,128]{2,0,1:T(4,128)S(1)} %get-tuple-element.174, ...), kind=kLoop, calls=%fused_computation.90 | loop fusion | flops 2340864 | bytes 11386880 | tf_op jit(solution)/shard_map/add | solution.py:75
  38.2 1.3 %multiply_add_fusion.22 = (f32[4,254,128]{2,0,1:T(4,128)S(1)}, f32[4,254,128]{2,0,1:T(4,128)S(1)}, f32[4,254,128]{2,0,1:T(4,128)S(1)}, f32[4,254,128]{2,0,1:T(4,...) fusion(f32[4,246,128]{2,0,1:T(4,128)S(1)} %get-tuple-element.166, ...), kind=kLoop, calls=%fused_computation.84 | loop fusion | flops 2340864 | bytes 11329536 | tf_op jit(solution)/shard_map/add | solution.py:75
  40.5 1.2 %multiply_add_fusion.20 = (f32[4,254,128]{2,0,1:T(4,128)S(1)}, f32[4,254,128]{2,0,1:T(4,128)S(1)}, f32[4,254,128]{2,0,1:T(4,128)S(1)}, f32[4,254,128]{2,0,1:T(4,...) fusion(f32[4,238,128]{2,0,1:T(4,128)S(1)} %get-tuple-element.158, ...), kind=kLoop, calls=%fused_computation.78 | loop fusion | flops 2340864 | bytes 11214848 | tf_op jit(solution)/shard_map/add | solution.py:75
  42.8 1.1 multiply_add_fusion.18
  44.8 1.1 multiply_add_fusion.16
  46.2 1.1 multiply_add_fusion.8
  48.0 20.7 %all_gather.12 = f32[4,32,128]{2,0,1:T(4,128)S(1)} all-gather(f32[4,2,128]{2,0,1:T(4,128)S(1)} %pad_maximum_fusion.5), channel_id=1, replica_groups=mesh['gx'=16,'gy'=16] {'gx'}, dimensions={1}, use_global_device_ids=true | all-gather | bytes 69632 | tf_op jit(solution)/shard_map/all_gather | solution.py:144
  69.5 15.0 %all_gather.15 = f32[4,32,128]{2,0,1:T(4,128)S(1)} all-gather(f32[4,2,128]{2,0,1:T(4,128)S(1)} %pad_maximum_fusion.8), channel_id=1, replica_groups=mesh['gx'=16,'gy'=16] {'gx'}, dimensions={1}, use_global_device_ids=true | all-gather | bytes 69632 | tf_op jit(solution)/shard_map/all_gather | solution.py:143
  84.5 15.7 %all_gather.14 = f32[4,32,128]{2,0,1:T(4,128)S(1)} all-gather(f32[4,2,128]{2,0,1:T(4,128)S(1)} %pad_maximum_fusion.7), channel_id=1, replica_groups=mesh['gx'=16,'gy'=16] {'gx'}, dimensions={1}, use_global_device_ids=true | all-gather | bytes 69632 | tf_op jit(solution)/shard_map/all_gather | solution.py:142
  100.3 14.9 %all_gather.13 = f32[4,32,128]{2,0,1:T(4,128)S(1)} all-gather(f32[4,2,128]{2,0,1:T(4,128)S(1)} %pad_maximum_fusion.6), channel_id=1, replica_groups=mesh['gx'=16,'gy'=16] {'gx'}, dimensions={1}, use_global_device_ids=true | all-gather | bytes 69632 | tf_op jit(solution)/shard_map/all_gather | solution.py:141
  (128 shorter events, 13.4 us)
Async XLA Ops:
  1.4 20.1 %collective-permute-start.1 = (f32[4,2,128]{2,0,1:T(4,128)S(1)}, f32[4,2,128]{2,0,1:T(4,128)S(1)}, u32[]{:S(2)}, u32[]{:S(2)}) collective-permute-start(f32[4,2,128]{2,0,1:T(4,128)S(1)} %get-tuple-element.94), channel_id=1, source_target_pairs={{0,16},{16,32},{32,48},{48,64},{64,80},{80,96},{96,112},{112,128},... | collective-permute-start | bytes 12296 | tf_op jit(solution)/shard_map/ppermute | solution.py:15
  6.3 9.3 %copy-start.10 = (f32[3,4,256,128]{3,2,1,0:T(8,128)S(1)}, f32[3,4,256,128]{3,2,1,0:T(8,128)}, u32[]{:S(2)}) copy-start(f32[3,4,256,128]{3,2,1,0:T(8,128)} %param.4) | copy-start | bytes 4718596
  6.3 15.6 %collective-permute-start = (f32[4,2,128]{2,0,1:T(4,128)S(1)}, f32[4,2,128]{2,0,1:T(4,128)S(1)}, u32[]{:S(2)}, u32[]{:S(2)}) collective-permute-start(f32[4,2,128]{2,0,1:T(4,128)S(1)} %get-tuple-element.93), channel_id=1, source_target_pairs={{16,0},{32,16},{48,32},{64,48},{80,64},{96,80},{112,96},{128,112},... | collective-permute-start | bytes 12296 | tf_op jit(solution)/shard_map/ppermute | solution.py:17
  9.4 12.6 %collective-permute-start.2 = (f32[2,256,128]{2,0,1:T(2,128)}, f32[2,256,128]{2,0,1:T(2,128)S(1)}, u32[]{:S(2)}, u32[]{:S(2)}) collective-permute-start(f32[2,256,128]{2,0,1:T(2,128)} %get-tuple-element.90), channel_id=1, source_target_pairs={{1,0},{2,1},{3,2},{4,3},{5,4},{6,5},{7,6},{8,7},{9,8},{10,9},{11,1... | collective-permute-start | bytes 786440 | tf_op jit(solution)/shard_map/ppermute | solution.py:17
  14.3 10.1 %collective-permute-start.3 = (f32[2,256,128]{2,0,1:T(2,128)}, f32[2,256,128]{2,0,1:T(2,128)}, u32[]{:S(2)}, u32[]{:S(2)}) collective-permute-start(f32[2,256,128]{2,0,1:T(2,128)} %get-tuple-element.89), channel_id=1, source_target_pairs={{0,1},{1,2},{2,3},{3,4},{4,5},{5,6},{6,7},{7,8},{8,9},{9,10},{10,1... | collective-permute-start | bytes 786440 | tf_op jit(solution)/shard_map/ppermute | solution.py:15
  15.6 1.3 %copy-start.11 = (f32[4,256,128]{2,1,0:T(8,128)S(1)}, f32[4,256,128]{2,1,0:T(8,128)}, u32[]{:S(2)}) copy-start(f32[4,256,128]{2,1,0:T(8,128)} %param.5) | copy-start | bytes 1572868
  18.6 2.9 %copy-start = (f32[4,256,128]{2,1,0:T(8,128)S(1)}, f32[4,256,128]{2,1,0:T(8,128)}, u32[]{:S(2)}) copy-start(f32[4,256,128]{2,1,0:T(8,128)} %param.3) | copy-start | bytes 1572868
  21.5 3.0 %copy-start.1 = (f32[4,256,2]{2,0,1:T(4,128)S(1)}, f32[4,256,2]{2,0,1:T(4,128)}, u32[]{:S(2)}) copy-start(f32[4,256,2]{2,0,1:T(4,128)} %get-tuple-element.91) | copy-start | bytes 24580
  21.5 3.0 %copy-start.2 = (f32[4,256,2]{2,0,1:T(4,128)S(1)}, f32[4,256,2]{2,0,1:T(4,128)}, u32[]{:S(2)}) copy-start(f32[4,256,2]{2,0,1:T(4,128)} %get-tuple-element.92) | copy-start | bytes 24580
  21.5 3.0 %copy-start.3 = (f32[1,4,256,128]{3,2,1,0:T(8,128)S(1)}, f32[1,4,256,128]{3,2,1,0:T(8,128)}, u32[]{:S(2)}) copy-start(f32[1,4,256,128]{3,2,1,0:T(8,128)} %get-tuple-element.49) | copy-start | bytes 1572868
  29.1 1.0 copy-start.4
  29.1 1.2 %copy-start.5 = (f32[4,253,128]{2,0,1:T(4,128)S(1)}, f32[4,253,128]{2,0,1:T(4,128)}, u32[]{:S(2)}) copy-start(f32[4,253,128]{2,0,1:T(4,128)} %get-tuple-element.225) | copy-start | bytes 1554436
  31.2 1.0 copy-start.6
  31.2 1.2 %copy-start.7 = (f32[4,253,128]{2,0,1:T(4,128)S(1)}, f32[4,253,128]{2,0,1:T(4,128)}, u32[]{:S(2)}) copy-start(f32[4,253,128]{2,0,1:T(4,128)} %get-tuple-element.226) | copy-start | bytes 1554436
  31.2 1.3 %copy-start.8 = (f32[4,253,128]{2,0,1:T(4,128)S(1)}, f32[4,253,128]{2,0,1:T(4,128)}, u32[]{:S(2)}) copy-start(f32[4,253,128]{2,0,1:T(4,128)} %get-tuple-element.227) | copy-start | bytes 1554436
  31.3 1.5 %copy-start.9 = (f32[4,253,128]{2,0,1:T(4,128)S(1)}, f32[4,253,128]{2,0,1:T(4,128)}, u32[]{:S(2)}) copy-start(f32[4,253,128]{2,0,1:T(4,128)} %pad_slice_fusion.11) | copy-start | bytes 1554436
where the time goes:
time: 118 us; the launch traced here: 117 us
  blocking collectives  66.3 us (56%)
  other arithmetic  18.4 us (16%)
  local copies, waits for them, and re-layouts  17.5 us (15%)
  starting transfers between devices  11.9 us (10%)
  waiting for transfers between devices  2.44 us (2%)
    all_gather x1, blocking collectives, shards(): lax.all_gather(reduced_right, 'gx', axis=1, tiled=True)  20.7 us
    all_gather x1, blocking collectives, shards(): lax.all_gather(reduced_diag, 'gx', axis=1, tiled=True)  15.7 us
    all_gather x1, blocking collectives, shards(): lax.all_gather(reduced_super, 'gx', axis=1, tiled=True)  15 us
    all_gather x1, blocking collectives, shards(): lax.all_gather(reduced_sub, 'gx', axis=1, tiled=True)  14.9 us
    add x11, other arithmetic, combine_rows(): value + factor_low * lower_value + factor_high * upper_value  9.81 us
    ppermute x2, starting transfers between devices, padded_2(): lax.ppermute(head, axis, [((i + 1) % count, i) for i in range(ends)])  6.98 us
    ppermute x2, starting transfers between devices, padded_2(): lax.ppermute(tail, axis, [(i, (i + 1) % count) for i in range(ends)])  4.93 us
    add x1, other arithmetic, build_rhs(): field - transport + 0.05 * (curve_y + curve_z)  4.7 us
  transfers between devices with their start and end apart: 4, of which 1 were waited for; matrix products, arithmetic and copies ran while one was open for 7% of the time, Pallas kernels for 0%

commit v1 on v0

--- a/solution.py
+++ b/solution.py
@@ -138,7 +138,9 @@
     reduced_super = jnp.concatenate([super_first, super_last], 1)
     reduced_right = jnp.concatenate([right_first, right_last], 1)
     gathered_lower_band, gathered_diagonal, gathered_upper_band, gathered_rhs = (
-        lax.all_gather(reduced_sub, "gx", axis=1, tiled=True),
+        jnp.concatenate(
+            lax.all_to_all(jnp.stack([reduced_sub] * lax.axis_size("gx")), "gx", 0, 0), axis=1
+        ),
         lax.all_gather(reduced_diag, "gx", axis=1, tiled=True),
         lax.all_gather(reduced_super, "gx", axis=1, tiled=True),
         lax.all_gather(reduced_right, "gx", axis=1, tiled=True),

time: 118 us -> 116 us (0.983)
  blocking collectives: 66.3 us -> 51.4 us
  waiting for transfers between devices: 2.44 us -> 10.2 us
  starting transfers between devices: 11.9 us -> 16.9 us
    all_gather x1 -> x0, blocking collectives: 14.9 us -> none  [shards(): lax.all_gather(reduced_sub, 'gx', axis=1, tiled=True)]
    all_to_all x0 -> x1, waiting for transfers between devices: none -> 7.75 us  [shards(): lax.all_to_all(jnp.stack([reduced_sub] * lax.axis_size('gx')), 'gx', 0, 0)]
    all_to_all x0 -> x1, starting transfers between devices: none -> 5.03 us  [shards(): lax.all_to_all(jnp.stack([reduced_sub] * lax.axis_size('gx')), 'gx', 0, 0)]
  transfers between devices with their start and end apart: 4 -> 5, of which waited for: 1 -> 2; matrix products, arithmetic and copies ran while one was open for 7% -> 7% of each run, Pallas kernels for 0% -> 0%
where the time goes in v1:
time: 116 us
  blocking collectives  51.4 us (44%)
  other arithmetic  18.4 us (16%)
  local copies, waits for them, and re-layouts  18.2 us (16%)
  starting transfers between devices  16.9 us (15%)
  waiting for transfers between devices  10.2 us (9%)
    all_gather x1, blocking collectives, shards(): lax.all_gather(reduced_right, 'gx', axis=1, tiled=True)  20.7 us
    all_gather x1, blocking collectives, shards(): lax.all_gather(reduced_diag, 'gx', axis=1, tiled=True)  15.7 us
    all_gather x1, blocking collectives, shards(): lax.all_gather(reduced_super, 'gx', axis=1, tiled=True)  15 us
    add x11, other arithmetic, combine_rows(): value + factor_low * lower_value + factor_high * upper_value  9.65 us
    all_to_all x1, waiting for transfers between devices, shards(): lax.all_to_all(jnp.stack([reduced_sub] * lax.axis_size('gx')), 'gx', 0, 0)  7.75 us
    ppermute x2, starting transfers between devices, padded_2(): lax.ppermute(head, axis, [((i + 1) % count, i) for i in range(ends)])  6.98 us
    all_to_all x1, starting transfers between devices, shards(): lax.all_to_all(jnp.stack([reduced_sub] * lax.axis_size('gx')), 'gx', 0, 0)  5.03 us
    ppermute x2, starting transfers between devices, padded_2(): lax.ppermute(tail, axis, [(i, (i + 1) % count) for i in range(ends)])  4.93 us
  transfers between devices with their start and end apart: 5, of which 2 were waited for; matrix products, arithmetic and copies ran while one was open for 7% of the time, Pallas kernels for 0%

profile of v1, /device:TPU:1, one launch (start us, length us, event | category | flops | bytes accessed | tf_op | source)
XLA Modules:
  0.0 115.9 jit_solution(6585161057471781886)
XLA Ops:
  0.0 1.4 %copy.19 = f32[4,256,128]{2,0,1:T(4,128)S(1)} copy(f32[4,256,128]{2,1,0:T(8,128)} %param.3) | data formatting | bytes 1048576 | tf_op args[0]
  1.4 4.9 %collective-permute-start.1 = (f32[4,2,128]{2,0,1:T(4,128)S(1)}, f32[4,2,128]{2,0,1:T(4,128)S(1)}, u32[]{:S(2)}, u32[]{:S(2)}) collective-permute-start(f32[4,2,128]{2,0,1:T(4,128)S(1)} %get-tuple-element.94), channel_id=1, source_target_pairs={{0,16},{16,32},{32,48},{48,64},{64,80},{80,96},{96,112},{112,128},... | collective-permute-start | bytes 12296 | tf_op jit(solution)/shard_map/ppermute | solution.py:15
  6.3 2.1 %collective-permute-start = (f32[4,2,128]{2,0,1:T(4,128)S(1)}, f32[4,2,128]{2,0,1:T(4,128)S(1)}, u32[]{:S(2)}, u32[]{:S(2)}) collective-permute-start(f32[4,2,128]{2,0,1:T(4,128)S(1)} %get-tuple-element.93), channel_id=1, source_target_pairs={{16,0},{32,16},{48,32},{64,48},{80,64},{96,80},{112,96},{128,112},... | collective-permute-start | bytes 12296 | tf_op jit(solution)/shard_map/ppermute | solution.py:17
  8.4 1.0 fusion.36
  9.4 4.9 %collective-permute-start.2 = (f32[2,256,128]{2,0,1:T(2,128)}, f32[2,256,128]{2,0,1:T(2,128)S(1)}, u32[]{:S(2)}, u32[]{:S(2)}) collective-permute-start(f32[2,256,128]{2,0,1:T(2,128)} %get-tuple-element.90), channel_id=1, source_target_pairs={{1,0},{2,1},{3,2},{4,3},{5,4},{6,5},{7,6},{8,7},{9,8},{10,9},{11,1... | collective-permute-start | bytes 786440 | tf_op jit(solution)/shard_map/ppermute | solution.py:17
  14.4 1.3 %fusion.37 = (f32[4,256,2]{2,0,1:T(4,128)}, f32[4,256,2]{2,0,1:T(4,128)}) fusion(f32[4,256,128]{2,0,1:T(4,128)S(1)} %copy.19), kind=kLoop, calls=%fused_computation.178 | loop fusion | bytes 32768 | tf_op jit(solution)/shard_map/slice | solution.py:37
  15.6 1.2 %fusion.32 = (f32[1,4,256,128]{3,2,1,0:T(8,128)}, f32[1,4,256,128]{3,2,1,0:T(8,128)}, f32[1,4,256,128]{3,2,1,0:T(8,128)}) fusion(f32[3,4,256,128]{3,2,1,0:T(8,128)S(1)} %copy-done.10), kind=kLoop, calls=%fused_computation.173 | loop fusion | bytes 3145728 | tf_op jit(solution)/shard_map/slice | solution.py:41
  17.4 1.3 %fusion.33 = (f32[4,253,128]{2,0,1:T(4,128)S(1)}, f32[4,253,128]{2,0,1:T(4,128)S(1)}, f32[4,253,128]{2,0,1:T(4,128)}, f32[4,253,128]{2,0,1:T(4,128)}) fusion(f32[4,256,128]{2,0,1:T(4,128)S(1)} %get-tuple-element.85, f32[4,256,128]{2,0,1:T(4,128)S(1)} %get-tuple-element.86), kind=kLoop, calls=%fused_computation.174 | loop fusion | bytes 4145152 | tf_op jit(solution)/shard_map/slice | solution.py:119
  19.5 1.1 pad_slice_fusion.8
  22.0 2.4 %collective-permute-done.3 = f32[2,256,128]{2,0,1:T(2,128)} collective-permute-done((f32[2,256,128]{2,0,1:T(2,128)}, f32[2,256,128]{2,0,1:T(2,128)}, u32[]{:S(2)}, u32[]{:S(2)}) %collective-permute-start.3) | collective-permute-done | bytes 262176 | tf_op jit(solution)/shard_map/ppermute | solution.py:15
  24.4 4.7 %fusion.11 = f32[4,256,128]{2,0,1:T(4,128)S(1)} fusion(f32[4,256,128]{2,0,1:T(4,128)S(1)} %copy.19, f32[4,258,128]{2,0,1:T(4,128)S(1)} %get-tuple-element.96, f32[4,258,128]{2,0,1:T(4,128)S(1)} %constant_dynamic-update-slice_fusion, f32[1,4,256,128]{3,2,1,0:T(8,128)} %get-tuple-element.51, f32[1,4,256,128]{3,2,1,0:T(8,128)} %get-tuple-element.50, ...), kind=kLoop, calls=%fused_computation.28 | loop fusion | flops 6291456 | bytes 5259264 | tf_op jit(solution)/shard_map/add | solution.py:42
  29.3 0.9 copy-done.4
  32.8 1.8 %multiply_add_fusion.26 = (f32[4,254,128]{2,0,1:T(4,128)S(1)}, f32[4,254,128]{2,0,1:T(4,128)S(1)}, f32[4,254,128]{2,0,1:T(4,128)S(1)}, f32[4,254,128]{2,0,1:T(4,...) fusion(f32[4,252,128]{2,0,1:T(4,128)S(1)} %get-tuple-element.178, ...), kind=kLoop, calls=%fused_computation.96 | loop fusion | flops 2340864 | bytes 9343992 | tf_op jit(solution)/shard_map/add | solution.py:75
  35.7 1.3 %multiply_add_fusion.24 = (f32[4,254,128]{2,0,1:T(4,128)S(1)}, f32[4,254,128]{2,0,1:T(4,128)S(1)}, f32[4,254,128]{2,0,1:T(4,128)S(1)}, f32[4,254,128]{2,0,1:T(4,...) fusion(f32[4,250,128]{2,0,1:T(4,128)S(1)} %get-tuple-element.174, ...), kind=kLoop, calls=%fused_computation.90 | loop fusion | flops 2340864 | bytes 11386880 | tf_op jit(solution)/shard_map/add | solution.py:75
  38.1 1.2 %multiply_add_fusion.22 = (f32[4,254,128]{2,0,1:T(4,128)S(1)}, f32[4,254,128]{2,0,1:T(4,128)S(1)}, f32[4,254,128]{2,0,1:T(4,128)S(1)}, f32[4,254,128]{2,0,1:T(4,...) fusion(f32[4,246,128]{2,0,1:T(4,128)S(1)} %get-tuple-element.166, ...), kind=kLoop, calls=%fused_computation.84 | loop fusion | flops 2340864 | bytes 11329536 | tf_op jit(solution)/shard_map/add | solution.py:75
  40.5 1.2 %multiply_add_fusion.20 = (f32[4,254,128]{2,0,1:T(4,128)S(1)}, f32[4,254,128]{2,0,1:T(4,128)S(1)}, f32[4,254,128]{2,0,1:T(4,128)S(1)}, f32[4,254,128]{2,0,1:T(4,...) fusion(f32[4,238,128]{2,0,1:T(4,128)S(1)} %get-tuple-element.158, ...), kind=kLoop, calls=%fused_computation.78 | loop fusion | flops 2340864 | bytes 11214848 | tf_op jit(solution)/shard_map/add | solution.py:75
  42.7 1.1 multiply_add_fusion.18
  44.7 1.1 multiply_add_fusion.16
  46.2 1.0 multiply_add_fusion.8
  47.9 20.7 %all_gather.9 = f32[4,32,128]{2,0,1:T(4,128)S(1)} all-gather(f32[4,2,128]{2,0,1:T(4,128)S(1)} %pad_maximum_fusion.5), channel_id=1, replica_groups=mesh['gx'=16,'gy'=16] {'gx'}, dimensions={1}, use_global_device_ids=true | all-gather | bytes 69632 | tf_op jit(solution)/shard_map/all_gather | solution.py:146
  69.4 15.0 %all_gather.11 = f32[4,32,128]{2,0,1:T(4,128)S(1)} all-gather(f32[4,2,128]{2,0,1:T(4,128)S(1)} %pad_maximum_fusion.8), channel_id=1, replica_groups=mesh['gx'=16,'gy'=16] {'gx'}, dimensions={1}, use_global_device_ids=true | all-gather | bytes 69632 | tf_op jit(solution)/shard_map/all_gather | solution.py:145
  84.4 15.7 %all_gather.10 = f32[4,32,128]{2,0,1:T(4,128)S(1)} all-gather(f32[4,2,128]{2,0,1:T(4,128)S(1)} %pad_maximum_fusion.7), channel_id=1, replica_groups=mesh['gx'=16,'gy'=16] {'gx'}, dimensions={1}, use_global_device_ids=true | all-gather | bytes 69632 | tf_op jit(solution)/shard_map/all_gather | solution.py:144
  100.8 5.0 %all-to-all-start = ((f32[16,4,2,128]{3,2,1,0:T(2,128)}), f32[16,4,2,128]{3,2,1,0:T(2,128)S(1)}, u32[]{:S(2)}, u32[]{:S(2)}) async-start(f32[16,4,2,128]{3,2,1,0:T(2,128)} %stack.2), calls=%async_computation | async-start | bytes 131072 | tf_op jit(solution)/shard_map/all_to_all | solution.py:142
  105.9 7.8 %all-to-all-done = f32[16,4,2,128]{3,2,1,0:T(2,128)S(1)} async-done(((f32[16,4,2,128]{3,2,1,0:T(2,128)}), f32[16,4,2,128]{3,2,1,0:T(2,128)S(1)}, u32[]{:S(2)}, u32[]{:S(2)}) %all-to-all-start) | async-done | bytes 65568 | tf_op jit(solution)/shard_map/all_to_all | solution.py:142
  (132 shorter events, 15.0 us)
Async XLA Ops:
  1.4 20.1 %collective-permute-start.1 = (f32[4,2,128]{2,0,1:T(4,128)S(1)}, f32[4,2,128]{2,0,1:T(4,128)S(1)}, u32[]{:S(2)}, u32[]{:S(2)}) collective-permute-start(f32[4,2,128]{2,0,1:T(4,128)S(1)} %get-tuple-element.94), channel_id=1, source_target_pairs={{0,16},{16,32},{32,48},{48,64},{64,80},{80,96},{96,112},{112,128},... | collective-permute-start | bytes 12296 | tf_op jit(solution)/shard_map/ppermute | solution.py:15
  6.3 9.3 %copy-start.10 = (f32[3,4,256,128]{3,2,1,0:T(8,128)S(1)}, f32[3,4,256,128]{3,2,1,0:T(8,128)}, u32[]{:S(2)}) copy-start(f32[3,4,256,128]{3,2,1,0:T(8,128)} %param.4) | copy-start | bytes 4718596
  6.3 15.6 %collective-permute-start = (f32[4,2,128]{2,0,1:T(4,128)S(1)}, f32[4,2,128]{2,0,1:T(4,128)S(1)}, u32[]{:S(2)}, u32[]{:S(2)}) collective-permute-start(f32[4,2,128]{2,0,1:T(4,128)S(1)} %get-tuple-element.93), channel_id=1, source_target_pairs={{16,0},{32,16},{48,32},{64,48},{80,64},{96,80},{112,96},{128,112},... | collective-permute-start | bytes 12296 | tf_op jit(solution)/shard_map/ppermute | solution.py:17
  9.4 12.6 %collective-permute-start.2 = (f32[2,256,128]{2,0,1:T(2,128)}, f32[2,256,128]{2,0,1:T(2,128)S(1)}, u32[]{:S(2)}, u32[]{:S(2)}) collective-permute-start(f32[2,256,128]{2,0,1:T(2,128)} %get-tuple-element.90), channel_id=1, source_target_pairs={{1,0},{2,1},{3,2},{4,3},{5,4},{6,5},{7,6},{8,7},{9,8},{10,9},{11,1... | collective-permute-start | bytes 786440 | tf_op jit(solution)/shard_map/ppermute | solution.py:17
  14.3 10.1 %collective-permute-start.3 = (f32[2,256,128]{2,0,1:T(2,128)}, f32[2,256,128]{2,0,1:T(2,128)}, u32[]{:S(2)}, u32[]{:S(2)}) collective-permute-start(f32[2,256,128]{2,0,1:T(2,128)} %get-tuple-element.89), channel_id=1, source_target_pairs={{0,1},{1,2},{2,3},{3,4},{4,5},{5,6},{6,7},{7,8},{8,9},{9,10},{10,1... | collective-permute-start | bytes 786440 | tf_op jit(solution)/shard_map/ppermute | solution.py:15
  15.6 1.3 %copy-start.11 = (f32[4,256,128]{2,1,0:T(8,128)S(1)}, f32[4,256,128]{2,1,0:T(8,128)}, u32[]{:S(2)}) copy-start(f32[4,256,128]{2,1,0:T(8,128)} %param.5) | copy-start | bytes 1572868
  18.7 2.9 %copy-start = (f32[4,256,128]{2,1,0:T(8,128)S(1)}, f32[4,256,128]{2,1,0:T(8,128)}, u32[]{:S(2)}) copy-start(f32[4,256,128]{2,1,0:T(8,128)} %param.3) | copy-start | bytes 1572868
  21.5 3.0 %copy-start.1 = (f32[4,256,2]{2,0,1:T(4,128)S(1)}, f32[4,256,2]{2,0,1:T(4,128)}, u32[]{:S(2)}) copy-start(f32[4,256,2]{2,0,1:T(4,128)} %get-tuple-element.91) | copy-start | bytes 24580
  21.5 3.0 %copy-start.2 = (f32[4,256,2]{2,0,1:T(4,128)S(1)}, f32[4,256,2]{2,0,1:T(4,128)}, u32[]{:S(2)}) copy-start(f32[4,256,2]{2,0,1:T(4,128)} %get-tuple-element.92) | copy-start | bytes 24580
  21.5 3.0 %copy-start.3 = (f32[1,4,256,128]{3,2,1,0:T(8,128)S(1)}, f32[1,4,256,128]{3,2,1,0:T(8,128)}, u32[]{:S(2)}) copy-start(f32[1,4,256,128]{3,2,1,0:T(8,128)} %get-tuple-element.49) | copy-start | bytes 1572868
  29.2 1.0 copy-start.4
  29.2 1.2 %copy-start.5 = (f32[4,253,128]{2,0,1:T(4,128)S(1)}, f32[4,253,128]{2,0,1:T(4,128)}, u32[]{:S(2)}) copy-start(f32[4,253,128]{2,0,1:T(4,128)} %get-tuple-element.225) | copy-start | bytes 1554436
  31.2 1.0 copy-start.6
  31.3 1.2 %copy-start.7 = (f32[4,253,128]{2,0,1:T(4,128)S(1)}, f32[4,253,128]{2,0,1:T(4,128)}, u32[]{:S(2)}) copy-start(f32[4,253,128]{2,0,1:T(4,128)} %get-tuple-element.226) | copy-start | bytes 1554436
  31.3 1.3 %copy-start.8 = (f32[4,253,128]{2,0,1:T(4,128)S(1)}, f32[4,253,128]{2,0,1:T(4,128)}, u32[]{:S(2)}) copy-start(f32[4,253,128]{2,0,1:T(4,128)} %get-tuple-element.227) | copy-start | bytes 1554436
  31.3 1.5 %copy-start.9 = (f32[4,253,128]{2,0,1:T(4,128)S(1)}, f32[4,253,128]{2,0,1:T(4,128)}, u32[]{:S(2)}) copy-start(f32[4,253,128]{2,0,1:T(4,128)} %pad_slice_fusion.11) | copy-start | bytes 1554436
  100.8 12.8 %all-to-all-start = ((f32[16,4,2,128]{3,2,1,0:T(2,128)}), f32[16,4,2,128]{3,2,1,0:T(2,128)S(1)}, u32[]{:S(2)}, u32[]{:S(2)}) async-start(f32[16,4,2,128]{3,2,1,0:T(2,128)} %stack.2), calls=%async_computation | async-start | bytes 131072 | tf_op jit(solution)/shard_map/all_to_all | solution.py:142
